TPU v7x, 32 devices: a whole 2x2x4 slice. The times are simulated.
32 devices in a mesh: nets: 8 (over z, x), region: 4 (over y, core).
Axes of the slice: x: 2, y: 2, z: 4, core: 2. Of those that a mesh axis runs over, the one named last changes fastest.
Arguments:
- logits: float32 [8192, 256], P('nets'), may hold values from -24 to 465
- tile_values: bfloat16 [8, 4, 384, 128, 128], P('nets', 'region'), may hold values from 0 to 1
- tile_pattern: int32 [8, 4, 384], P('nets', 'region'), may hold values from 0 to 2047
- tile_edge: int32 [8, 4, 384], P('nets', 'region'), may hold values from 0 to 63
- tile_counts: int32 [8, 4, 8], P('nets', 'region'), may hold values from 12 to 48, as said below
- capacity: int32 [4, 65536], P('region', 'nets'), may hold values from 0 to 2
Outputs:
- logit_grad: float32 [8192, 256], P('nets')
- usage: float32 [4, 65536], P('region', 'nets')
Inputs may be any that keep to these rules, and one draw needn't show every extreme that they name: `tile_counts`: each entry is at most 48; in every draw some owner receives 48 live slots from every group of a region, and every group has a full owner in every region.
All inputs are finite; a program needn't handle non-finite values.
Results may differ from a plain program's by a relative error of at most 0.0011.
Values may be sent and summed in bfloat16 or wider, within the bound.
No kernel may reach another device: no remote copies, remote signals or barrier semaphores. Data moves between devices by JAX's collectives and lax.ppermute only.
A program may use at most 64 MiB of HBM per device.

v0:
```python
import jax
import jax.numpy as jnp
from jax import lax
from jax.sharding import PartitionSpec as P


def shards(logits, tile_values, tile_pattern, tile_edge, tile_counts, capacity):
    groups = lax.axis_size("nets")
    tile_block = tile_values[0, 0]
    tile_count = tile_block.shape[0]
    block_size = tile_block.shape[1]
    slot_count = tile_count // groups
    pattern_idx = tile_pattern[0, 0]
    edge_idx = tile_edge[0, 0]
    counts = tile_counts[0, 0]
    live_slot = (jnp.arange(slot_count, dtype=jnp.int32)[None, :] < counts[:, None]).reshape(
        tile_count
    )
    weight_live = live_slot.astype(jnp.float32)
    probs = jax.nn.softmax(logits, axis=-1)
    probs_half = probs.astype(jnp.bfloat16).reshape(-1, block_size)
    picked = probs_half[pattern_idx]
    contrib = (
        jnp.einsum("tq,tqe->te", picked, tile_block, preferred_element_type=jnp.float32)
        * weight_live[:, None]
    )
    capacity_f = capacity.reshape(-1, block_size).astype(jnp.float32)
    owned_blocks = capacity_f.shape[0]
    owner_idx = jnp.arange(tile_count, dtype=jnp.int32) // slot_count
    target = owner_idx * owned_blocks + edge_idx
    partial_value = (
        jnp.zeros((groups * owned_blocks, block_size), jnp.float32).at[target].add(contrib)
    )
    usage_edges = lax.psum_scatter(partial_value, "nets", scatter_dimension=0, tiled=True)
    edge_grad = jax.nn.sigmoid(usage_edges - capacity_f).astype(jnp.bfloat16)
    all_grads = lax.all_gather(edge_grad, "nets", axis=0, tiled=True)
    slot_grads = all_grads[target]
    dp_tiles = (
        jnp.einsum("tqe,te->tq", tile_block, slot_grads, preferred_element_type=jnp.float32)
        * weight_live[:, None]
    )
    local_grad = (
        jnp.zeros((probs_half.shape[0], block_size), jnp.float32).at[pattern_idx].add(dp_tiles)
    )
    summed_grad = lax.psum(local_grad.reshape(logits.shape), "region")
    logit_grad = probs * (summed_grad - jnp.sum(probs * summed_grad, axis=-1, keepdims=True))
    return (logit_grad, usage_edges.reshape(capacity.shape))


def solution(mesh):
    in_specs = (
        P("nets", None),
        P("nets", "region", None, None, None),
        P("nets", "region", None),
        P("nets", "region", None),
        P("nets", "region", None),
        P("region", "nets"),
    )
    out_specs = (P("nets", None), P("region", "nets"))
    return jax.shard_map(shards, mesh=mesh, in_specs=in_specs, out_specs=out_specs, check_vma=False)
```

profile of v0, /device:TPU:0, one launch (start us, length us, event | category | flops | bytes accessed | tf_op | source)
XLA Modules:
  0.0 181.0 jit_solution(4683535861114849851)
XLA Ops:
  7.2 0.0 reduce-scatter.2.cloned.1.call-start
  7.2 0.7 fusion.17
  7.9 0.7 fusion.18
  8.6 1.4 reduce_max.9
  10.1 1.6 fusion.5
  11.7 0.7 fusion.16
  12.4 0.1 reshape.122
  12.5 1.6 fusion.21
  14.0 0.0 copy-start.1
  14.1 0.2 reshape.119
  14.2 1.4 gather_fusion
  15.7 6.4 %fusion.2 = f32[384,1,128]{2,1,0:T(1,128)S(1)} fusion(bf16[1,1,384,128,128]{4,3,2,1,0:T(8,128)(2,1)} %param.7, bf16[384,128,1]{1,0,2:T(8,128)(2,1)S(1)} %bitcast.18), kind=kOutput, calls=%fused_computation.6 | convolution fusion | flops 12582912 | bytes 12877824 | tf_op jit(solution)/shard_map/tq,tqe->te/dot_general | solution.py:24
  22.1 0.0 copy-start
  22.1 2.6 %scatter_custom_fusion = f32[512,128]{1,0:T(8,128)} fusion(s32[384]{0:T(512)S(1)} %fusion.18, f32[384,128]{1,0:T(8,128)S(1)} %bitcast.19, f32[]{:T(128)} %constant.11.clone.1, f32[384]{0:T(512)S(1)} %reshape.122), kind=kCustom, calls=%fused_computation.18 | custom fusion | flops 98304 | bytes 460804 | tf_op jit(solution)/shard_map/scatter-add | solution.py:32
  24.7 0.0 reduce-scatter.2.cloned.1.call-update
  24.7 0.0 all-reduce.2.cloned.1.call-start
  24.8 0.0 copy-done.1
  24.8 64.0 %reduce-scatter.2.cloned.1.call-done = f32[64,128]{1,0:T(8,128)} async-done(((f32[512,128]{1,0:T(8,128)}), f32[64,128]{1,0:T(8,128)}) %reduce-scatter.2.cloned.1.call-update) | async-done | bytes 32784 | tf_op jit(solution)/shard_map/reduce_scatter | solution.py:34
  88.8 0.8 divide_convert_fusion
  89.6 30.5 %all_gather.3 = bf16[512,128]{1,0:T(8,128)(2,1)S(1)} all-gather(bf16[64,128]{1,0:T(8,128)(2,1)S(1)} %divide_convert_fusion), channel_id=1, replica_groups=mesh['nets'=8,'region'=4] {'nets'}, dimensions={0}, use_global_device_ids=true | all-gather | bytes 147456 | tf_op jit(solution)/shard_map/all_gather | solution.py:36
  120.1 1.4 gather_fusion.1
  121.6 9.5 %fusion = f32[384,1,128]{2,1,0:T(1,128)S(1)} fusion(bf16[1,1,384,128,128]{4,3,2,1,0:T(8,128)(2,1)} %param.7, bf16[384,128,1]{1,0,2:T(8,128)(2,1)S(1)} %bitcast.20), kind=kOutput, calls=%fused_computation.4 | convolution fusion | flops 12582912 | bytes 12877824 | tf_op jit(solution)/shard_map/tqe,te->tq/dot_general | solution.py:39
  131.0 2.2 %scatter_custom_fusion.1 = f32[2048,128]{1,0:T(8,128)S(1)} fusion(s32[384]{0:T(512)S(1)} %fusion.17, f32[]{:T(128)} %constant.11.clone.1, f32[384,128]{1,0:T(8,128)S(1)} %bitcast.21, f32[384]{0:T(512)S(1)} %reshape.122), kind=kCustom, calls=%fused_computation.13 | custom fusion | flops 98304 | bytes 1247236 | tf_op jit(solution)/shard_map/scatter-add | solution.py:43
  133.2 1.3 reshape.120
  134.5 0.0 all-reduce.2.cloned.1.call-update
  134.5 35.3 %all-reduce.2.cloned.1.call-done = f32[1024,256]{1,0:T(8,128)} async-done(((f32[1024,256]{1,0:T(8,128)}), f32[1024,256]{1,0:T(8,128)}) %all-reduce.2.cloned.1.call-update) | async-done | bytes 1048592 | tf_op jit(solution)/shard_map/psum | solution.py:45
  169.8 0.0 copy-done
  169.8 1.7 multiply_reduce_fusion
  171.5 2.7 %subtract_multiply_fusion = f32[1024,256]{1,0:T(8,128)} fusion(f32[1024,256]{1,0:T(8,128)} %all-reduce.2.cloned.1.call-done, f32[1024]{0:T(1024)S(1)} %multiply_reduce_fusion, f32[1024]{0:T(1024)S(1)} %fusion.5, f32[1024,256]{1,0:T(8,128)S(1)} %copy-done, f32[1024]{0:T(1024)S(1)} %reduce_max.9), kind=kLoop, calls=%fused_computation.8 | loop fusion | flops 1048576 | bytes 3158016 | tf_op jit(solution)/shard_map/mul | solution.py:46
  (3 shorter events, 0.0 us)
Async XLA Ops:
  7.2 81.6 %reduce-scatter.2.cloned.1.call-start = ((), (), s32[]{:S(2)}) async-start(), calls=%async_computation.1 | async-start | bytes 294912 | tf_op jit(solution)/shard_map/reduce_scatter | solution.py:34
  14.0 10.7 %copy-start.1 = (s32[1,8192]{1,0:T(1,128)S(1)}, s32[1,8192]{1,0:T(1,128)}, u32[]{:S(2)}) copy-start(s32[1,8192]{1,0:T(1,128)} %param.11) | copy-start | bytes 98308
  22.1 147.8 %copy-start = (f32[1024,256]{1,0:T(8,128)S(1)}, f32[1024,256]{1,0:T(8,128)}, u32[]{:S(2)}) copy-start(f32[1024,256]{1,0:T(8,128)} %param.6) | copy-start | bytes 3145732
  24.7 145.1 %all-reduce.2.cloned.1.call-start = ((), (), s32[]{:S(2)}) async-start(), calls=%async_computation.2 | async-start | bytes 2097152 | tf_op jit(solution)/shard_map/psum | solution.py:45
Sparse Core Ops, SparseCore 0:
  24.8 63.9 reduce-scatter.1
  134.7 35.0 all-reduce.1
where the time goes:
time: 181 us
  waiting for transfers between devices  99.3 us (55%)
  blocking collectives  30.5 us (17%)
  other arithmetic  16.8 us (9%)
  matrix products  15.8 us (9%)
  between operations  14.1 us (8%)
  local copies, waits for them, and re-layouts  4.42 us (2%)
    reduce_scatter x1, waiting for transfers between devices, shards(): lax.psum_scatter(partial_value, 'nets', scatter_dimension=0, tiled=True)  64 us
    psum x1, waiting for transfers between devices, shards(): summed_grad = lax.psum(local_grad.reshape(logits.shape), 'region')  35.3 us
    all_gather x1, blocking collectives, shards(): all_grads = lax.all_gather(edge_grad, 'nets', axis=0, tiled=True)  30.5 us
    dot_general x1, matrix products, shards(): jnp.einsum('tqe,te->tq', tile_block, slot_grads, preferred_element_type=j...  9.46 us
    dot_general x1, matrix products, shards(): jnp.einsum('tq,tqe->te', picked, tile_block, preferred_element_type=jnp.f...  6.35 us
  transfers between devices with their start and end apart: 2, of which 2 were waited for; matrix products, arithmetic and copies ran while one was open for 0% of the time, Pallas kernels for 0%

commit v1 on v0

--- a/solution.py
+++ b/solution.py
@@ -33,7 +33,17 @@
     )
     usage_edges = lax.psum_scatter(partial_value, "nets", scatter_dimension=0, tiled=True)
     edge_grad = jax.nn.sigmoid(usage_edges - capacity_f).astype(jnp.bfloat16)
-    all_grads = lax.all_gather(edge_grad, "nets", axis=0, tiled=True)
+    world = lax.axis_size("nets")
+    known = [(i0 - 1, i0) for i0 in range(1, world)] + [(world - 1, 0)]
+    a_now = edge_grad
+    panels = [a_now]
+    dev_i = 0
+    while dev_i < world - 1:
+        a_now = lax.ppermute(a_now, "nets", known)
+        panels += [a_now]
+        dev_i = dev_i + 1
+    all_rows = jnp.concatenate([*reversed(panels)], axis=0)
+    all_grads = jnp.roll(all_rows, (lax.axis_index("nets") + 1) * a_now.shape[0], axis=0)
     slot_grads = all_grads[target]
     dp_tiles = (
         jnp.einsum("tqe,te->tq", tile_block, slot_grads, preferred_element_type=jnp.float32)

time: 181 us -> 195 us (1.077)
  waiting for transfers between devices: 99.3 us -> 141 us
  blocking collectives: 30.5 us -> 0 us
    ppermute x0 -> x7, waiting for transfers between devices: none -> 43.7 us  [shards(): a_now = lax.ppermute(a_now, 'nets', known)]
    all_gather x1 -> x0, blocking collectives: 30.5 us -> none  [shards(): all_grads = lax.all_gather(edge_grad, 'nets', axis=0, tiled=True)]
  transfers between devices with their start and end apart: 2 -> 9, of which waited for: 2 -> 9; matrix products, arithmetic and copies ran while one was open for 0% -> 0% of each run, Pallas kernels for 0% -> 0%
where the time goes in v1:
time: 195 us; the launch traced here: 194 us
  waiting for transfers between devices  141 us (72%)
  other arithmetic  16.8 us (9%)
  matrix products  15.8 us (8%)
  between operations  14.2 us (7%)
  local copies, waits for them, and re-layouts  4.58 us (2%)
    reduce_scatter x1, waiting for transfers between devices, shards(): lax.psum_scatter(partial_value, 'nets', scatter_dimension=0, tiled=True)  64 us
    ppermute x7, waiting for transfers between devices, shards(): a_now = lax.ppermute(a_now, 'nets', known)  43.7 us
    psum x1, waiting for transfers between devices, shards(): summed_grad = lax.psum(local_grad.reshape(logits.shape), 'region')  33.4 us
    dot_general x1, matrix products, shards(): jnp.einsum('tqe,te->tq', tile_block, slot_grads, preferred_element_type=j...  9.46 us
    dot_general x1, matrix products, shards(): jnp.einsum('tq,tqe->te', picked, tile_block, preferred_element_type=jnp.f...  6.35 us
  transfers between devices with their start and end apart: 9, of which 9 were waited for; matrix products, arithmetic and copies ran while one was open for 0% of the time, Pallas kernels for 0%

profile of v1, /device:TPU:0, one launch (start us, length us, event | category | flops | bytes accessed | tf_op | source)
XLA Modules:
  0.0 194.2 jit_solution(6581640028289121096)
XLA Ops:
  7.2 0.0 reduce-scatter.2.cloned.1.call-start
  7.2 0.7 fusion.17
  7.9 0.7 fusion.18
  8.6 1.4 reduce_max.9
  10.1 1.6 fusion.5
  11.7 0.7 fusion.16
  12.4 0.1 reshape.122
  12.5 1.6 fusion.21
  14.0 0.0 copy-start.1
  14.1 0.2 reshape.119
  14.2 1.4 gather_fusion
  15.7 6.4 %fusion.2 = f32[384,1,128]{2,1,0:T(1,128)S(1)} fusion(bf16[1,1,384,128,128]{4,3,2,1,0:T(8,128)(2,1)} %param.7, bf16[384,128,1]{1,0,2:T(8,128)(2,1)S(1)} %bitcast.18), kind=kOutput, calls=%fused_computation.6 | convolution fusion | flops 12582912 | bytes 12877824 | tf_op jit(solution)/shard_map/tq,tqe->te/dot_general | solution.py:24
  22.1 0.0 copy-start
  22.1 2.6 %scatter_custom_fusion = f32[512,128]{1,0:T(8,128)} fusion(s32[384]{0:T(512)S(1)} %fusion.18, f32[384,128]{1,0:T(8,128)S(1)} %bitcast.19, f32[]{:T(128)} %constant.22.clone.1, f32[384]{0:T(512)S(1)} %reshape.122), kind=kCustom, calls=%fused_computation.18 | custom fusion | flops 98304 | bytes 460804 | tf_op jit(solution)/shard_map/scatter-add | solution.py:32
  24.7 0.0 reduce-scatter.2.cloned.1.call-update
  24.7 0.0 all-reduce.2.cloned.1.call-start
  24.8 0.0 copy-done.1
  24.8 64.0 %reduce-scatter.2.cloned.1.call-done = f32[64,128]{1,0:T(8,128)} async-done(((f32[512,128]{1,0:T(8,128)}), f32[64,128]{1,0:T(8,128)}) %reduce-scatter.2.cloned.1.call-update) | async-done | bytes 32784 | tf_op jit(solution)/shard_map/reduce_scatter | solution.py:34
  88.8 0.8 divide_convert_fusion
  89.6 1.5 collective-permute-start
  91.1 5.0 %collective-permute-done = bf16[64,128]{1,0:T(8,128)(2,1)S(1)} collective-permute-done((bf16[64,128]{1,0:T(8,128)(2,1)S(1)}, bf16[64,128]{1,0:T(8,128)(2,1)S(1)}, u32[]{:S(2)}, u32[]{:S(2)}) %collective-permute-start) | collective-permute-done | bytes 16416 | tf_op jit(solution)/shard_map/ppermute | solution.py:42
  96.1 0.0 collective-permute-start.1
  96.1 6.4 %collective-permute-done.1 = bf16[64,128]{1,0:T(8,128)(2,1)S(1)} collective-permute-done((bf16[64,128]{1,0:T(8,128)(2,1)S(1)}, bf16[64,128]{1,0:T(8,128)(2,1)S(1)}, u32[]{:S(2)}, u32[]{:S(2)}) %collective-permute-start.1) | collective-permute-done | bytes 16416 | tf_op jit(solution)/shard_map/ppermute | solution.py:42
  102.5 0.0 collective-permute-start.2
  102.5 6.6 %collective-permute-done.2 = bf16[64,128]{1,0:T(8,128)(2,1)S(1)} collective-permute-done((bf16[64,128]{1,0:T(8,128)(2,1)S(1)}, bf16[64,128]{1,0:T(8,128)(2,1)S(1)}, u32[]{:S(2)}, u32[]{:S(2)}) %collective-permute-start.2) | collective-permute-done | bytes 16416 | tf_op jit(solution)/shard_map/ppermute | solution.py:42
  109.1 0.0 collective-permute-start.3
  109.1 6.4 %collective-permute-done.3 = bf16[64,128]{1,0:T(8,128)(2,1)S(1)} collective-permute-done((bf16[64,128]{1,0:T(8,128)(2,1)S(1)}, bf16[64,128]{1,0:T(8,128)(2,1)S(1)}, u32[]{:S(2)}, u32[]{:S(2)}) %collective-permute-start.3) | collective-permute-done | bytes 16416 | tf_op jit(solution)/shard_map/ppermute | solution.py:42
  115.5 0.0 collective-permute-start.4
  115.5 6.4 %collective-permute-done.4 = bf16[64,128]{1,0:T(8,128)(2,1)S(1)} collective-permute-done((bf16[64,128]{1,0:T(8,128)(2,1)S(1)}, bf16[64,128]{1,0:T(8,128)(2,1)S(1)}, u32[]{:S(2)}, u32[]{:S(2)}) %collective-permute-start.4) | collective-permute-done | bytes 16416 | tf_op jit(solution)/shard_map/ppermute | solution.py:42
  121.9 0.0 collective-permute-start.5
  121.9 6.4 %collective-permute-done.5 = bf16[64,128]{1,0:T(8,128)(2,1)S(1)} collective-permute-done((bf16[64,128]{1,0:T(8,128)(2,1)S(1)}, bf16[64,128]{1,0:T(8,128)(2,1)S(1)}, u32[]{:S(2)}, u32[]{:S(2)}) %collective-permute-start.5) | collective-permute-done | bytes 16416 | tf_op jit(solution)/shard_map/ppermute | solution.py:42
  128.4 0.0 collective-permute-start.6
  128.4 6.4 %collective-permute-done.6 = bf16[64,128]{1,0:T(8,128)(2,1)S(1)} collective-permute-done((bf16[64,128]{1,0:T(8,128)(2,1)S(1)}, bf16[64,128]{1,0:T(8,128)(2,1)S(1)}, u32[]{:S(2)}, u32[]{:S(2)}) %collective-permute-start.6) | collective-permute-done | bytes 16416 | tf_op jit(solution)/shard_map/ppermute | solution.py:42
  135.0 1.4 gather_fusion.1
  136.5 9.5 %fusion = f32[384,1,128]{2,1,0:T(1,128)S(1)} fusion(bf16[1,1,384,128,128]{4,3,2,1,0:T(8,128)(2,1)} %param.7, bf16[384,128,1]{1,0,2:T(8,128)(2,1)S(1)} %bitcast.20), kind=kOutput, calls=%fused_computation.4 | convolution fusion | flops 12582912 | bytes 12877824 | tf_op jit(solution)/shard_map/tqe,te->tq/dot_general | solution.py:49
  145.9 2.2 %scatter_custom_fusion.1 = f32[2048,128]{1,0:T(8,128)S(1)} fusion(s32[384]{0:T(512)S(1)} %fusion.17, f32[]{:T(128)} %constant.22.clone.1, f32[384,128]{1,0:T(8,128)S(1)} %bitcast.21, f32[384]{0:T(512)S(1)} %reshape.122), kind=kCustom, calls=%fused_computation.13 | custom fusion | flops 98304 | bytes 1247236 | tf_op jit(solution)/shard_map/scatter-add | solution.py:53
  148.2 1.3 reshape.120
  149.4 0.0 all-reduce.2.cloned.1.call-update
  149.5 33.4 %all-reduce.2.cloned.1.call-done = f32[1024,256]{1,0:T(8,128)} async-done(((f32[1024,256]{1,0:T(8,128)}), f32[1024,256]{1,0:T(8,128)}) %all-reduce.2.cloned.1.call-update) | async-done | bytes 1048592 | tf_op jit(solution)/shard_map/psum | solution.py:55
  182.9 0.0 copy-done
  182.9 1.7 multiply_reduce_fusion
  184.6 2.7 %subtract_multiply_fusion = f32[1024,256]{1,0:T(8,128)} fusion(f32[1024,256]{1,0:T(8,128)} %all-reduce.2.cloned.1.call-done, f32[1024]{0:T(1024)S(1)} %multiply_reduce_fusion, f32[1024]{0:T(1024)S(1)} %fusion.5, f32[1024,256]{1,0:T(8,128)S(1)} %copy-done, f32[1024]{0:T(1024)S(1)} %reduce_max.9), kind=kLoop, calls=%fused_computation.8 | loop fusion | flops 1048576 | bytes 3158016 | tf_op jit(solution)/shard_map/mul | solution.py:56
  (20 shorter events, 0.2 us)
Async XLA Ops:
  7.2 81.6 %reduce-scatter.2.cloned.1.call-start = ((), (), s32[]{:S(2)}) async-start(), calls=%async_computation.1 | async-start | bytes 294912 | tf_op jit(solution)/shard_map/reduce_scatter | solution.py:34
  14.0 10.7 %copy-start.1 = (s32[1,8192]{1,0:T(1,128)S(1)}, s32[1,8192]{1,0:T(1,128)}, u32[]{:S(2)}) copy-start(s32[1,8192]{1,0:T(1,128)} %param.11) | copy-start | bytes 98308
  22.1 160.9 %copy-start = (f32[1024,256]{1,0:T(8,128)S(1)}, f32[1024,256]{1,0:T(8,128)}, u32[]{:S(2)}) copy-start(f32[1024,256]{1,0:T(8,128)} %param.6) | copy-start | bytes 3145732
  24.7 158.2 %all-reduce.2.cloned.1.call-start = ((), (), s32[]{:S(2)}) async-start(), calls=%async_computation.2 | async-start | bytes 2097152 | tf_op jit(solution)/shard_map/psum | solution.py:55
  89.6 6.5 %collective-permute-start = (bf16[64,128]{1,0:T(8,128)(2,1)S(1)}, bf16[64,128]{1,0:T(8,128)(2,1)S(1)}, u32[]{:S(2)}, u32[]{:S(2)}) collective-permute-start(bf16[64,128]{1,0:T(8,128)(2,1)S(1)} %divide_convert_fusion), channel_id=1, source_target_pairs={{0,4},{4,8},{8,12},{12,16},{16,20},{20,24},{24,28},{28,0},{1,5},{5... | collective-permute-start | bytes 49160 | tf_op jit(solution)/shard_map/ppermute | solution.py:42
  96.1 6.4 %collective-permute-start.1 = (bf16[64,128]{1,0:T(8,128)(2,1)S(1)}, bf16[64,128]{1,0:T(8,128)(2,1)S(1)}, u32[]{:S(2)}, u32[]{:S(2)}) collective-permute-start(bf16[64,128]{1,0:T(8,128)(2,1)S(1)} %collective-permute-done), channel_id=1, source_target_pairs={{0,4},{4,8},{8,12},{12,16},{16,20},{20,24},{24,28},{28,0},{1,5},{5... | collective-permute-start | bytes 49160 | tf_op jit(solution)/shard_map/ppermute | solution.py:42
  102.5 6.6 %collective-permute-start.2 = (bf16[64,128]{1,0:T(8,128)(2,1)S(1)}, bf16[64,128]{1,0:T(8,128)(2,1)S(1)}, u32[]{:S(2)}, u32[]{:S(2)}) collective-permute-start(bf16[64,128]{1,0:T(8,128)(2,1)S(1)} %collective-permute-done.1), channel_id=1, source_target_pairs={{0,4},{4,8},{8,12},{12,16},{16,20},{20,24},{24,28},{28,0},{1,5},{5... | collective-permute-start | bytes 49160 | tf_op jit(solution)/shard_map/ppermute | solution.py:42
  109.1 6.4 %collective-permute-start.3 = (bf16[64,128]{1,0:T(8,128)(2,1)S(1)}, bf16[64,128]{1,0:T(8,128)(2,1)S(1)}, u32[]{:S(2)}, u32[]{:S(2)}) collective-permute-start(bf16[64,128]{1,0:T(8,128)(2,1)S(1)} %collective-permute-done.2), channel_id=1, source_target_pairs={{0,4},{4,8},{8,12},{12,16},{16,20},{20,24},{24,28},{28,0},{1,5},{5... | collective-permute-start | bytes 49160 | tf_op jit(solution)/shard_map/ppermute | solution.py:42
  115.5 6.4 %collective-permute-start.4 = (bf16[64,128]{1,0:T(8,128)(2,1)S(1)}, bf16[64,128]{1,0:T(8,128)(2,1)S(1)}, u32[]{:S(2)}, u32[]{:S(2)}) collective-permute-start(bf16[64,128]{1,0:T(8,128)(2,1)S(1)} %collective-permute-done.3), channel_id=1, source_target_pairs={{0,4},{4,8},{8,12},{12,16},{16,20},{20,24},{24,28},{28,0},{1,5},{5... | collective-permute-start | bytes 49160 | tf_op jit(solution)/shard_map/ppermute | solution.py:42
  121.9 6.4 %collective-permute-start.5 = (bf16[64,128]{1,0:T(8,128)(2,1)S(1)}, bf16[64,128]{1,0:T(8,128)(2,1)S(1)}, u32[]{:S(2)}, u32[]{:S(2)}) collective-permute-start(bf16[64,128]{1,0:T(8,128)(2,1)S(1)} %collective-permute-done.4), channel_id=1, source_target_pairs={{0,4},{4,8},{8,12},{12,16},{16,20},{20,24},{24,28},{28,0},{1,5},{5... | collective-permute-start | bytes 49160 | tf_op jit(solution)/shard_map/ppermute | solution.py:42
  128.4 6.4 %collective-permute-start.6 = (bf16[64,128]{1,0:T(8,128)(2,1)S(1)}, bf16[64,128]{1,0:T(8,128)(2,1)S(1)}, u32[]{:S(2)}, u32[]{:S(2)}) collective-permute-start(bf16[64,128]{1,0:T(8,128)(2,1)S(1)} %collective-permute-done.5), channel_id=1, source_target_pairs={{0,4},{4,8},{8,12},{12,16},{16,20},{20,24},{24,28},{28,0},{1,5},{5... | collective-permute-start | bytes 49160 | tf_op jit(solution)/shard_map/ppermute | solution.py:42
Sparse Core Ops, SparseCore 0:
  24.8 63.9 reduce-scatter.1
  149.6 33.2 all-reduce.1
